TPU v7x, 128 devices: a whole 4x4x4 slice. The times are simulated.
128 devices in a mesh: rep: 4 (over x), fsdp: 2 (over core), tp: 16 (over z, y).
Axes of the slice: x: 4, y: 4, z: 4, core: 2. Of those that a mesh axis runs over, the one named last changes fastest.
Arguments:
- tokens: bfloat16 [8192, 2048], P(('rep', 'fsdp'), 'tp'), may hold values from -6 to 6
- cotangent: bfloat16 [8192, 2048], P(('rep', 'fsdp'), 'tp'), may hold values from -6 to 6
- frame_mask: int32 [8192], P(('rep', 'fsdp')), may hold values 0 or 1
- ln_gain: bfloat16 [2048], P('tp'), may hold values from 0.099609375 to 1.8984375
- ln_bias: bfloat16 [2048], P('tp'), may hold values from -3 to 3
- weight_in: bfloat16 [2048, 8192], P('fsdp', 'tp'), may hold values from -0.1875 to 0.1875
- weight_out: bfloat16 [8192, 2048], P('tp', 'fsdp'), may hold values from -0.09375 to 0.09375
- blocks_in: int32 [16, 64], P('fsdp', 'tp'), may hold values 0 or 1
- blocks_out: int32 [64, 16], P('tp', 'fsdp'), may hold values 0 or 1
Outputs:
- block_out: bfloat16 [8192, 2048], P(('rep', 'fsdp'), 'tp')
- input_grad: bfloat16 [8192, 2048], P(('rep', 'fsdp'), 'tp')
- grad_in: float32 [2048, 8192], P('fsdp', 'tp')
- grad_out: float32 [8192, 2048], P('tp', 'fsdp')
- grad_gain: float32 [2048], P('tp')
- grad_bias: float32 [2048], P('tp')
All inputs are finite; a program needn't handle non-finite values. No bound on the sum of `frame_mask` or of `blocks_in` or of `blocks_out` on one device may be relied on, other than what follows from the above.
Results may differ from a plain program's by a relative error of at most 0.019.
Values may be sent and summed in bfloat16 or wider, within the bound.
No kernel may reach another device: no remote copies, remote signals or barrier semaphores. Data moves between devices by JAX's collectives and lax.ppermute only.
A program may use at most 128 MiB of HBM per device.

v0:
```python
from functools import partial
import jax
import jax.numpy as jnp
from jax import lax
from jax.sharding import PartitionSpec as P

BLK = 128


def apply_blocks(weight, blocks, kind):
    row_blocks, col_blocks = blocks.shape
    shaped = weight.reshape(row_blocks, BLK, col_blocks, BLK)
    keeper = blocks.astype(kind)[:, None, :, None]
    return (shaped * keeper).reshape(weight.shape)


def contract_rows(left, right):
    return lax.dot_general(
        left, right, (((0,), (0,)), ((), ())), preferred_element_type=jnp.float32
    )


def contract_cols(left, right):
    return lax.dot_general(
        left, right, (((1,), (1,)), ((), ())), preferred_element_type=jnp.float32
    )


def on_device(
    tokens, cotangent, frame_mask, ln_gain, ln_bias, weight_in, weight_out, blocks_in, blocks_out
):
    whole_rows, whole_grad, gain_full, bias_full = (
        lax.all_gather(tokens, "tp", axis=1, tiled=True),
        lax.all_gather(cotangent, "tp", axis=1, tiled=True),
        lax.all_gather(ln_gain, "tp", axis=0, tiled=True),
        lax.all_gather(ln_bias, "tp", axis=0, tiled=True),
    )
    masked_in = apply_blocks(weight_in, blocks_in, jnp.bfloat16)
    masked_out = apply_blocks(weight_out, blocks_out, jnp.bfloat16)
    full_in, full_out = (
        lax.all_gather(masked_in, "fsdp", axis=0, tiled=True),
        lax.all_gather(masked_out, "fsdp", axis=1, tiled=True),
    )
    width = whole_rows.shape[1]
    own_width = tokens.shape[1]
    col_start = lax.axis_index("tp") * own_width
    gelu_exact = partial(jax.nn.gelu, approximate=False)
    values = whole_rows.astype(jnp.float32)
    centre = jnp.mean(values, axis=1, keepdims=True)
    centred = values - centre
    inv_std = lax.rsqrt(jnp.mean(centred * centred, axis=1, keepdims=True) + 1e-05)
    normed = centred * inv_std
    scaled = (normed * gain_full.astype(jnp.float32) + bias_full.astype(jnp.float32)).astype(
        jnp.bfloat16
    )
    hidden = jnp.dot(scaled, full_in, preferred_element_type=jnp.float32)
    active = gelu_exact(hidden).astype(jnp.bfloat16)
    partial_out = jnp.dot(active, full_out, preferred_element_type=jnp.float32)
    branch = lax.psum_scatter(
        partial_out.astype(jnp.bfloat16), "tp", scatter_dimension=1, tiled=True
    ).astype(jnp.float32)
    block_out = (tokens.astype(jnp.float32) + branch).astype(jnp.bfloat16)
    flags = frame_mask[:, None].astype(jnp.bfloat16)
    chosen = whole_grad * flags
    chosen_own = cotangent * flags
    back_active = contract_cols(chosen, full_out)
    unused, gelu_back = jax.vjp(gelu_exact, hidden)
    back_hidden = gelu_back(back_active)[0].astype(jnp.bfloat16)
    partial_normed = contract_cols(back_hidden, full_in)
    normed_own = lax.dynamic_slice_in_dim(normed, col_start, own_width, 1)
    gain_own = ln_gain.astype(jnp.float32)
    back_normed = lax.psum_scatter(
        partial_normed.astype(jnp.bfloat16), "tp", scatter_dimension=1, tiled=True
    ).astype(jnp.float32)
    back_scaled = back_normed * gain_own
    sum_plain = jnp.sum(back_scaled, axis=1)
    sum_cross = jnp.sum(back_scaled * normed_own, axis=1)
    sum_plain, sum_cross = lax.psum((sum_plain, sum_cross), "tp")
    mean_plain = (sum_plain / width)[:, None]
    mean_cross = (sum_cross / width)[:, None]
    back_rows = inv_std * (back_scaled - mean_plain - normed_own * mean_cross)
    input_grad = (chosen_own.astype(jnp.float32) + back_rows).astype(jnp.bfloat16)
    local_gain = jnp.sum(back_normed * normed_own, axis=0)
    local_bias = jnp.sum(back_normed, axis=0)
    grad_gain, grad_bias = lax.psum((local_gain, local_bias), ("rep", "fsdp"))
    term_in = contract_rows(scaled, back_hidden)
    term_out = contract_rows(active, chosen)
    shard_in, shard_out = (
        lax.psum_scatter(
            term_in.astype(jnp.bfloat16), "fsdp", scatter_dimension=0, tiled=True
        ).astype(jnp.float32),
        lax.psum_scatter(
            term_out.astype(jnp.bfloat16), "fsdp", scatter_dimension=1, tiled=True
        ).astype(jnp.float32),
    )
    shard_in, shard_out = (
        lax.psum(shard_in.astype(jnp.bfloat16), "rep").astype(jnp.float32),
        lax.psum(shard_out.astype(jnp.bfloat16), "rep").astype(jnp.float32),
    )
    grad_in = apply_blocks(shard_in, blocks_in, jnp.float32)
    grad_out = apply_blocks(shard_out, blocks_out, jnp.float32)
    return (block_out, input_grad, grad_in, grad_out, grad_gain, grad_bias)


def solution(mesh):
    placed = (
        P(("rep", "fsdp"), "tp"),
        P(("rep", "fsdp"), "tp"),
        P(("rep", "fsdp")),
        P("tp"),
        P("tp"),
        P("fsdp", "tp"),
        P("tp", "fsdp"),
        P("fsdp", "tp"),
        P("tp", "fsdp"),
    )
    return jax.shard_map(
        on_device,
        mesh=mesh,
        in_specs=placed,
        out_specs=(
            P(("rep", "fsdp"), "tp"),
            P(("rep", "fsdp"), "tp"),
            P("fsdp", "tp"),
            P("tp", "fsdp"),
            P("tp"),
            P("tp"),
        ),
        check_vma=False,
    )
```

profile of v0, /device:TPU:0, one launch (start us, length us, event | category | flops | bytes accessed | tf_op | source)
XLA Modules:
  0.0 492.1 jit_solution(3719068611543885792)
XLA Ops:
  7.2 0.7 all-gather.7.cloned.1.call-update
  7.9 0.8 fusion.34
  8.7 0.1 copy.17
  8.8 0.3 mul.149
  9.2 2.4 bitcast_multiply_fusion.3
  11.7 0.2 mul.155
  12.0 1.2 bitcast_multiply_fusion.2
  13.2 0.5 all-gather.13.cloned.1.call-update
  13.8 22.1 %all-gather = bf16[16,1,128]{2,1,0:T(2,128)(2,1)S(1)} all-gather(bf16[1,1,128]{2,1,0:T(2,128)(2,1)S(1)} %bitcast.45), channel_id=1, replica_groups=mesh['rep'=4,'fsdp'=2,'tp'=16] {'tp'}, dimensions={0}, use_global_device_ids=true | all-gather | bytes 4352 | tf_op jit(solution)/shard_map/all_gather | solution.py:35
  36.0 19.5 %all-gather.1 = bf16[16,1,128]{2,1,0:T(2,128)(2,1)S(1)} all-gather(bf16[1,1,128]{2,1,0:T(2,128)(2,1)S(1)} %bitcast.44), channel_id=1, replica_groups=mesh['rep'=4,'fsdp'=2,'tp'=16] {'tp'}, dimensions={0}, use_global_device_ids=true | all-gather | bytes 4352 | tf_op jit(solution)/shard_map/all_gather | solution.py:36
  55.5 14.8 %all-gather.7.cloned.1.call-done = bf16[1024,2048]{1,0:T(8,128)(2,1)} async-done(((bf16[1024,128]{1,0:T(8,128)(2,1)}), bf16[1024,2048]{1,0:T(8,128)(2,1)}) %all-gather.7.cloned.1.call-update) | async-done | bytes 4194320 | tf_op jit(solution)/shard_map/all_gather | solution.py:33
  70.4 3.0 convert_reduce_fusion
  73.4 0.5 copy-done
  73.8 1.2 fusion.2
  75.1 10.1 %all-gather.9.cloned.1.call-done = bf16[2048,512]{1,0:T(8,128)(2,1)} async-done(((bf16[1024,512]{1,0:T(8,128)(2,1)}), bf16[2048,512]{1,0:T(8,128)(2,1)}) %all-gather.9.cloned.1.call-update) | async-done | bytes 2097168 | tf_op jit(solution)/shard_map/all_gather | solution.py:41
  85.1 10.5 %multiply_convert_fusion = (bf16[1024,512]{1,0:T(8,128)(2,1)S(1)}, f32[1024,512]{1,0:T(8,128)}, f32[1024,512]{1,0:T(8,128)}) fusion(bf16[2048,512]{1,0:T(8,128)(2,1)} %all-gather.9.cloned.1.call-done, f32[2048]{0:T(1024)S(1)} %bitcast.42, f32[2048]{0:T(1024)S(1)} %bitcast.40, f32[1024]{0:T(1024)S(1)} %add_rsqrt_fusion, ...), kind=kOutput, calls=%fused_computation.21 | convolution fusion | flops 2194145280 | bytes 11558912 | tf_op jit(solution)/shard_map/dot_general | solution.py:56
  95.6 5.8 %all-gather.11.cloned.1.call-done = bf16[512,2048]{1,0:T(8,128)(2,1)} async-done(((bf16[512,1024]{1,0:T(8,128)(2,1)}), bf16[512,2048]{1,0:T(8,128)(2,1)}) %all-gather.11.cloned.1.call-update) | async-done | bytes 2097168 | tf_op jit(solution)/shard_map/all_gather | solution.py:42
  101.4 61.1 %all-gather.13.cloned.1.call-done = bf16[1024,2048]{1,0:T(8,128)(2,1)} async-done(((bf16[1024,128]{1,0:T(8,128)(2,1)}), bf16[1024,2048]{1,0:T(8,128)(2,1)}) %all-gather.13.cloned.1.call-update) | async-done | bytes 4194320 | tf_op jit(solution)/shard_map/all_gather | solution.py:34
  162.5 7.1 %add_convert_fusion.1 = bf16[1024,512]{1,0:T(8,128)(2,1)S(1)} fusion(f32[1024,512]{1,0:T(8,128)} %get-tuple-element.17, f32[1024,512]{1,0:T(8,128)} %get-tuple-element.22, bf16[512,2048]{1,0:T(8,128)(2,1)} %all-gather.11.cloned.1.call-done, bf16[1024,2048]{1,0:T(8,128)(2,1)} %all-gather.13.cloned.1.call-done, bf16[1024]{0:T(1024)(128)(2,1)S(1)} %convert_element_type.88), kind=kOutput, calls=%fused_computation.18 | convolution fusion | flops 2156920832 | bytes 11536384 | tf_op jit(solution)/shard_map/dot_general | solution.py:24
  169.7 1.0 copy-done.14
  170.7 4.4 convolution_convert_fusion.2
  175.1 0.2 reduce-scatter.11.cloned.1.call-start
  175.4 6.0 %fusion.7 = bf16[512,2048]{1,0:T(8,128)(2,1)} fusion(bf16[1024,512]{1,0:T(8,128)(2,1)S(1)} %get-tuple-element.16, bf16[1024,2048]{1,0:T(8,128)(2,1)} %all-gather.13.cloned.1.call-done, bf16[1024]{0:T(1024)(128)(2,1)S(1)} %convert_element_type.88), kind=kOutput, calls=%fused_computation.14 | convolution fusion | flops 2150629376 | bytes 7342080 | tf_op jit(solution)/shard_map/dot_general | solution.py:18
  181.4 5.3 %reduce-scatter.9.cloned.1.call-done = bf16[1024,512]{1,0:T(8,128)(2,1)} async-done(((bf16[2048,512]{1,0:T(8,128)(2,1)}), bf16[1024,512]{1,0:T(8,128)(2,1)}) %reduce-scatter.9.cloned.1.call-update) | async-done | bytes 1048592 | tf_op jit(solution)/shard_map/reduce_scatter | solution.py:89
  186.7 16.6 %reduce-scatter.11.cloned.1.call-done = bf16[512,1024]{1,0:T(8,128)(2,1)} async-done(((bf16[512,2048]{1,0:T(8,128)(2,1)}), bf16[512,1024]{1,0:T(8,128)(2,1)}) %reduce-scatter.11.cloned.1.call-update) | async-done | bytes 1048592 | tf_op jit(solution)/shard_map/reduce_scatter | solution.py:92
  203.4 5.5 %convolution_convert_fusion = bf16[1024,2048]{1,0:T(8,128)(2,1)} fusion(bf16[1024,512]{1,0:T(8,128)(2,1)} %copy-done.14, bf16[2048,512]{1,0:T(8,128)(2,1)S(1)} %copy-done.11), kind=kOutput, calls=%fused_computation.6 | convolution fusion | flops 2149580800 | bytes 7340032 | tf_op jit(solution)/shard_map/dot_general | solution.py:24
  208.9 6.4 %copy.21 = bf16[1024,2048]{0,1:T(8,128)(2,1)} copy(bf16[1024,2048]{1,0:T(8,128)(2,1)} %convolution_convert_fusion) | data formatting | bytes 8388608
  215.4 1.6 copy-done.12
  217.0 5.5 %convolution_convert_fusion.1 = bf16[1024,2048]{1,0:T(8,128)(2,1)} fusion(bf16[1024,512]{1,0:T(8,128)(2,1)} %copy-done.13, bf16[512,2048]{1,0:T(8,128)(2,1)S(1)} %copy-done.12), kind=kOutput, calls=%fused_computation.7 | convolution fusion | flops 2149580800 | bytes 7340032 | tf_op jit(solution)/shard_map/dot_general | solution.py:58
  222.5 6.4 %copy.19 = bf16[1024,2048]{0,1:T(8,128)(2,1)} copy(bf16[1024,2048]{1,0:T(8,128)(2,1)} %convolution_convert_fusion.1) | data formatting | bytes 8388608
  228.9 0.1 copy.18
  229.0 6.4 %fusion = f32[1024,2048]{1,0:T(8,128)} fusion(bf16[1024,2048]{1,0:T(8,128)(2,1)} %all-gather.7.cloned.1.call-done, f32[1024]{0:T(1024)S(1)} %add_rsqrt_fusion, f32[1024]{0:T(1024)S(1)} %broadcast_multiply_fusion.2), kind=kLoop, calls=%fused_computation.2 | loop fusion | flops 6291456 | bytes 12591104 | tf_op jit(solution)/shard_map/mul | solution.py:52
  235.4 30.6 %all-reduce.5.cloned.1.call-done = (bf16[1024,512]{1,0:T(8,128)(2,1)}, bf16[512,1024]{1,0:T(8,128)(2,1)}) async-done(((bf16[1024,512]{1,0:T(8,128)(2,1)}, bf16[512,1024]{1,0:T(8,128)(2,1)}), (bf16[1024,512]{1,0:T(8,128)(2,1)}, bf16[512,1024]{1,0:T(8,128)(2,1)})) %all-reduce.5.cloned.1.call-update) | async-done | bytes 2097168 | tf_op jit(solution)/shard_map/psum | solution.py:97
  266.0 0.3 mul.177
  266.4 0.9 copy-done.4
  267.3 1.7 bitcast_multiply_fusion.1
  268.9 0.2 mul.180
  269.1 1.0 copy-done.3
  270.2 2.0 bitcast_multiply_fusion
  272.2 75.3 %reduce-scatter.15.cloned.1.call-done = bf16[128,1024]{1,0:T(8,128)(2,1)} async-done(((bf16[2048,1024]{1,0:T(8,128)(2,1)}), bf16[128,1024]{1,0:T(8,128)(2,1)}) %reduce-scatter.15.cloned.1.call-update) | async-done | bytes 262160
  347.4 1.1 copy.22
  348.5 79.2 %reduce-scatter.13.cloned.1.call-done = bf16[128,1024]{1,0:T(8,128)(2,1)} async-done(((bf16[2048,1024]{1,0:T(8,128)(2,1)}), bf16[128,1024]{1,0:T(8,128)(2,1)}) %reduce-scatter.13.cloned.1.call-update) | async-done | bytes 262160
  427.7 1.1 copy.20
  428.8 0.8 add_convert_fusion.4
  429.6 1.4 fusion.29
  431.0 13.5 %all-reduce.1 = (f32[128]{0:T(128)}, f32[128]{0:T(128)}) all-reduce(f32[128]{0:T(128)S(1)} %get-tuple-element.6, f32[128]{0:T(128)S(1)} %get-tuple-element.9), channel_id=1, replica_groups=mesh['rep'=4,'fsdp'=2,'tp'=16] {'rep','fsdp'}, use_global_device_ids=true, to_apply=%region_13.0 | all-reduce | flops 256 | bytes 2048 | tf_op jit(solution)/shard_map/psum | solution.py:85
  444.5 38.7 %all-reduce = (f32[1024]{0:T(1024)S(1)}, f32[1024]{0:T(1024)S(1)}) all-reduce(f32[1024]{0:T(1024)S(1)} %get-tuple-element.7, f32[1024]{0:T(1024)S(1)} %get-tuple-element.8), channel_id=1, replica_groups=mesh['rep'=4,'fsdp'=2,'tp'=16] {'tp'}, use_global_device_ids=true, to_apply=%region_7.0 | all-reduce | flops 2048 | bytes 16384 | tf_op jit(solution)/shard_map/psum | solution.py:78
  483.2 2.4 fusion.27
  (48 shorter events, 0.5 us)
Async XLA Ops:
  7.2 63.2 %all-gather.7.cloned.1.call-start = ((), (), s32[]{:S(2)}) async-start(), calls=%async_computation.4 | async-start | bytes 4456448 | tf_op jit(solution)/shard_map/all_gather | solution.py:33
  7.9 77.2 %all-gather.9.cloned.1.call-start = ((), (), s32[]{:S(2)}) async-start(), calls=%async_computation.5 | async-start | bytes 3145728 | tf_op jit(solution)/shard_map/all_gather | solution.py:41
  9.2 2.5 copy-start.8
  9.2 2.7 copy-start.2
  11.6 89.8 %all-gather.11.cloned.1.call-start = ((), (), s32[]{:S(2)}) async-start(), calls=%async_computation.6 | async-start | bytes 3145728 | tf_op jit(solution)/shard_map/all_gather | solution.py:42
  11.9 1.9 copy-start.10
  11.9 24.1 %copy-start.9 = (bf16[128]{0:T(256)(128)(2,1)S(1)}, bf16[128]{0:T(256)(128)(2,1)}, u32[]{:S(2)}) copy-start(bf16[128]{0:T(256)(128)(2,1)} %param.13) | copy-start | bytes 772
  11.9 43.6 %copy-start.7 = (s32[1024]{0:T(1024)S(1)}, s32[1024]{0:T(1024)}, u32[]{:S(2)}) copy-start(s32[1024]{0:T(1024)} %param.11) | copy-start | bytes 12292
  13.2 149.3 %all-gather.13.cloned.1.call-start = ((), (), s32[]{:S(2)}) async-start(), calls=%async_computation.7 | async-start | bytes 4456448 | tf_op jit(solution)/shard_map/all_gather | solution.py:34
  13.8 173.0 %reduce-scatter.9.cloned.1.call-start = ((), (), s32[]{:S(2)}) async-start(), calls=%async_computation.8 | async-start | bytes 3145728 | tf_op jit(solution)/shard_map/reduce_scatter | solution.py:89
  70.4 3.4 copy-start
  95.6 79.8 %copy-start.13 = (bf16[1024,512]{1,0:T(8,128)(2,1)}, bf16[1024,512]{1,0:T(8,128)(2,1)S(1)}, u32[]{:S(2)}) copy-start(bf16[1024,512]{1,0:T(8,128)(2,1)S(1)} %get-tuple-element.16) | copy-start | bytes 3145732
  162.5 8.1 %copy-start.1 = (bf16[1024,2048]{1,0:T(8,128)(2,1)S(1)}, bf16[1024,2048]{1,0:T(8,128)(2,1)}, u32[]{:S(2)}) copy-start(bf16[1024,2048]{1,0:T(8,128)(2,1)} %all-gather.7.cloned.1.call-done) | copy-start | bytes 12582916
  169.6 1.0 copy-start.14
  175.1 28.2 %reduce-scatter.11.cloned.1.call-start = ((), (), s32[]{:S(2)}) async-start(), calls=%async_computation.9 | async-start | bytes 3145728 | tf_op jit(solution)/shard_map/reduce_scatter | solution.py:92
  181.3 22.1 %copy-start.11 = (bf16[2048,512]{1,0:T(8,128)(2,1)S(1)}, bf16[2048,512]{1,0:T(8,128)(2,1)}, u32[]{:S(2)}) copy-start(bf16[2048,512]{1,0:T(8,128)(2,1)} %all-gather.9.cloned.1.call-done) | copy-start | bytes 6291460
  181.4 84.7 %all-reduce.5.cloned.1.call-start = ((), (), s32[]{:S(2)}) async-start(), calls=%async_computation.12 | async-start | bytes 4194304 | tf_op jit(solution)/shard_map/psum | solution.py:97
  203.3 144.1 %reduce-scatter.15.cloned.1.call-start = ((), (), s32[]{:S(2)}) async-start(), calls=%async_computation.11 | async-start | bytes 4456448
  215.3 1.6 copy-start.12
  215.3 212.4 %reduce-scatter.13.cloned.1.call-start = ((), (), s32[]{:S(2)}) async-start(), calls=%async_computation.10 | async-start | bytes 4456448
  266.0 1.2 copy-start.4
  268.9 1.2 copy-start.3
  270.2 158.7 %copy-start.5 = (bf16[1024,128]{1,0:T(8,128)(2,1)S(1)}, bf16[1024,128]{1,0:T(8,128)(2,1)}, u32[]{:S(2)}) copy-start(bf16[1024,128]{1,0:T(8,128)(2,1)} %param.9) | copy-start | bytes 786436
  272.2 211.0 %copy-start.6 = (bf16[1024,128]{1,0:T(8,128)(2,1)S(1)}, bf16[1024,128]{1,0:T(8,128)(2,1)}, u32[]{:S(2)}) copy-start(bf16[1024,128]{1,0:T(8,128)(2,1)} %param.10) | copy-start | bytes 786436
Sparse Core Ops, SparseCore 0:
  10.1 60.2 all-gather.6
  72.6 12.4 all-gather.8
  86.8 14.6 all-gather.10
  103.4 59.0 all-gather.12
  175.2 11.4 reduce-scatter.8
  189.6 13.6 reduce-scatter.10
  205.8 60.2 all-reduce.4
  269.7 77.6 reduce-scatter.14
  350.8 76.9 reduce-scatter.12
where the time goes:
time: 493 us; the launch traced here: 492 us
  waiting for transfers between devices  300 us (61%)
  blocking collectives  93.8 us (19%)
  matrix products  39 us (8%)
  other arithmetic  23.2 us (5%)
  local copies, waits for them, and re-layouts  21.3 us (4%)
  between operations  14.1 us (3%)
    unnamed x11, waiting for transfers between devices  156 us
    all_gather x1, waiting for transfers between devices, on_device(): lax.all_gather(cotangent, 'tp', axis=1, tiled=True)  61.1 us
    psum x1, blocking collectives, on_device(): sum_plain, sum_cross = lax.psum((sum_plain, sum_cross), 'tp')  38.7 us
    psum x1, waiting for transfers between devices, on_device(): lax.psum(shard_in.astype(jnp.bfloat16), 'rep').astype(jnp.float32)  30.6 us
    all_gather x1, blocking collectives, on_device(): lax.all_gather(ln_gain, 'tp', axis=0, tiled=True)  22.1 us
    unnamed x34, local copies, waits for them, and re-layouts  20 us
    all_gather x1, blocking collectives, on_device(): lax.all_gather(ln_bias, 'tp', axis=0, tiled=True)  19.5 us
    reduce_scatter x1, waiting for transfers between devices, on_device(): lax.psum_scatter(term_out.astype(jnp.bfloat16), 'fsdp', scatter_dimension...  16.6 us
  transfers between devices with their start and end apart: 9, of which 9 were waited for; matrix products, arithmetic and copies ran while one was open for 12% of the time, Pallas kernels for 0%

commit v1 on v0

--- a/solution.py
+++ b/solution.py
@@ -5,6 +5,12 @@
 from jax.sharding import PartitionSpec as P
 
 BLK = 128
+
+
+def place_ways_here(payload, bus_axis, a_name):
+    for i in (bus_axis, a_name):
+        payload = lax.psum(payload, i)
+    return payload
 
 
 def apply_blocks(weight, blocks, kind):
@@ -82,7 +88,7 @@
     input_grad = (chosen_own.astype(jnp.float32) + back_rows).astype(jnp.bfloat16)
     local_gain = jnp.sum(back_normed * normed_own, axis=0)
     local_bias = jnp.sum(back_normed, axis=0)
-    grad_gain, grad_bias = lax.psum((local_gain, local_bias), ("rep", "fsdp"))
+    grad_gain, grad_bias = place_ways_here((local_gain, local_bias), "rep", "fsdp")
     term_in = contract_rows(scaled, back_hidden)
     term_out = contract_rows(active, chosen)
     shard_in, shard_out = (

time: 493 us -> 493 us (level)
    psum x1 -> x2, blocking collectives: 13.5 us -> 13.4 us  [place_ways_here(): payload = lax.psum(payload, i)]
where the time goes in v1:
time: 493 us; the launch traced here: 492 us
  waiting for transfers between devices  300 us (61%)
  blocking collectives  93.8 us (19%)
  matrix products  39 us (8%)
  other arithmetic  23.2 us (5%)
  local copies, waits for them, and re-layouts  21.3 us (4%)
  between operations  14.1 us (3%)
    unnamed x11, waiting for transfers between devices  156 us
    all_gather x1, waiting for transfers between devices, on_device(): lax.all_gather(cotangent, 'tp', axis=1, tiled=True)  61.1 us
    psum x1, blocking collectives, on_device(): sum_plain, sum_cross = lax.psum((sum_plain, sum_cross), 'tp')  38.7 us
    psum x1, waiting for transfers between devices, on_device(): lax.psum(shard_in.astype(jnp.bfloat16), 'rep').astype(jnp.float32)  30.6 us
    all_gather x1, blocking collectives, on_device(): lax.all_gather(ln_gain, 'tp', axis=0, tiled=True)  22.1 us
    unnamed x34, local copies, waits for them, and re-layouts  20 us
    all_gather x1, blocking collectives, on_device(): lax.all_gather(ln_bias, 'tp', axis=0, tiled=True)  19.5 us
    reduce_scatter x1, waiting for transfers between devices, on_device(): lax.psum_scatter(term_out.astype(jnp.bfloat16), 'fsdp', scatter_dimension...  16.6 us
  transfers between devices with their start and end apart: 9, of which 9 were waited for; matrix products, arithmetic and copies ran while one was open for 12% of the time, Pallas kernels for 0%

profile of v1, /device:TPU:0, one launch (start us, length us, event | category | flops | bytes accessed | tf_op | source)
XLA Modules:
  0.0 492.1 jit_solution(1459919132903715678)
XLA Ops:
  7.2 0.7 all-gather.7.cloned.1.call-update
  7.9 0.8 fusion.34
  8.7 0.1 copy.17
  8.8 0.3 mul.149
  9.2 2.4 bitcast_multiply_fusion.3
  11.7 0.2 mul.155
  12.0 1.2 bitcast_multiply_fusion.2
  13.2 0.5 all-gather.13.cloned.1.call-update
  13.8 22.1 %all-gather = bf16[16,1,128]{2,1,0:T(2,128)(2,1)S(1)} all-gather(bf16[1,1,128]{2,1,0:T(2,128)(2,1)S(1)} %bitcast.45), channel_id=1, replica_groups=mesh['rep'=4,'fsdp'=2,'tp'=16] {'tp'}, dimensions={0}, use_global_device_ids=true | all-gather | bytes 4352 | tf_op jit(solution)/shard_map/all_gather | solution.py:41
  36.0 19.5 %all-gather.1 = bf16[16,1,128]{2,1,0:T(2,128)(2,1)S(1)} all-gather(bf16[1,1,128]{2,1,0:T(2,128)(2,1)S(1)} %bitcast.44), channel_id=1, replica_groups=mesh['rep'=4,'fsdp'=2,'tp'=16] {'tp'}, dimensions={0}, use_global_device_ids=true | all-gather | bytes 4352 | tf_op jit(solution)/shard_map/all_gather | solution.py:42
  55.5 14.8 %all-gather.7.cloned.1.call-done = bf16[1024,2048]{1,0:T(8,128)(2,1)} async-done(((bf16[1024,128]{1,0:T(8,128)(2,1)}), bf16[1024,2048]{1,0:T(8,128)(2,1)}) %all-gather.7.cloned.1.call-update) | async-done | bytes 4194320 | tf_op jit(solution)/shard_map/all_gather | solution.py:39
  70.4 3.0 convert_reduce_fusion
  73.4 0.5 copy-done
  73.8 1.2 fusion.2
  75.1 10.1 %all-gather.9.cloned.1.call-done = bf16[2048,512]{1,0:T(8,128)(2,1)} async-done(((bf16[1024,512]{1,0:T(8,128)(2,1)}), bf16[2048,512]{1,0:T(8,128)(2,1)}) %all-gather.9.cloned.1.call-update) | async-done | bytes 2097168 | tf_op jit(solution)/shard_map/all_gather | solution.py:47
  85.1 10.5 %multiply_convert_fusion = (bf16[1024,512]{1,0:T(8,128)(2,1)S(1)}, f32[1024,512]{1,0:T(8,128)}, f32[1024,512]{1,0:T(8,128)}) fusion(bf16[2048,512]{1,0:T(8,128)(2,1)} %all-gather.9.cloned.1.call-done, f32[2048]{0:T(1024)S(1)} %bitcast.42, f32[2048]{0:T(1024)S(1)} %bitcast.40, f32[1024]{0:T(1024)S(1)} %add_rsqrt_fusion, ...), kind=kOutput, calls=%fused_computation.21 | convolution fusion | flops 2194145280 | bytes 11558912 | tf_op jit(solution)/shard_map/dot_general | solution.py:62
  95.6 5.8 %all-gather.11.cloned.1.call-done = bf16[512,2048]{1,0:T(8,128)(2,1)} async-done(((bf16[512,1024]{1,0:T(8,128)(2,1)}), bf16[512,2048]{1,0:T(8,128)(2,1)}) %all-gather.11.cloned.1.call-update) | async-done | bytes 2097168 | tf_op jit(solution)/shard_map/all_gather | solution.py:48
  101.4 61.1 %all-gather.13.cloned.1.call-done = bf16[1024,2048]{1,0:T(8,128)(2,1)} async-done(((bf16[1024,128]{1,0:T(8,128)(2,1)}), bf16[1024,2048]{1,0:T(8,128)(2,1)}) %all-gather.13.cloned.1.call-update) | async-done | bytes 4194320 | tf_op jit(solution)/shard_map/all_gather | solution.py:40
  162.5 7.1 %add_convert_fusion.1 = bf16[1024,512]{1,0:T(8,128)(2,1)S(1)} fusion(f32[1024,512]{1,0:T(8,128)} %get-tuple-element.19, f32[1024,512]{1,0:T(8,128)} %get-tuple-element.24, bf16[512,2048]{1,0:T(8,128)(2,1)} %all-gather.11.cloned.1.call-done, bf16[1024,2048]{1,0:T(8,128)(2,1)} %all-gather.13.cloned.1.call-done, bf16[1024]{0:T(1024)(128)(2,1)S(1)} %convert_element_type.88), kind=kOutput, calls=%fused_computation.18 | convolution fusion | flops 2156920832 | bytes 11536384 | tf_op jit(solution)/shard_map/dot_general | solution.py:30
  169.7 1.0 copy-done.14
  170.7 4.4 convolution_convert_fusion.2
  175.1 0.2 reduce-scatter.11.cloned.1.call-start
  175.4 6.0 %fusion.7 = bf16[512,2048]{1,0:T(8,128)(2,1)} fusion(bf16[1024,512]{1,0:T(8,128)(2,1)S(1)} %get-tuple-element.18, bf16[1024,2048]{1,0:T(8,128)(2,1)} %all-gather.13.cloned.1.call-done, bf16[1024]{0:T(1024)(128)(2,1)S(1)} %convert_element_type.88), kind=kOutput, calls=%fused_computation.14 | convolution fusion | flops 2150629376 | bytes 7342080 | tf_op jit(solution)/shard_map/dot_general | solution.py:24
  181.4 5.3 %reduce-scatter.9.cloned.1.call-done = bf16[1024,512]{1,0:T(8,128)(2,1)} async-done(((bf16[2048,512]{1,0:T(8,128)(2,1)}), bf16[1024,512]{1,0:T(8,128)(2,1)}) %reduce-scatter.9.cloned.1.call-update) | async-done | bytes 1048592 | tf_op jit(solution)/shard_map/reduce_scatter | solution.py:95
  186.7 16.6 %reduce-scatter.11.cloned.1.call-done = bf16[512,1024]{1,0:T(8,128)(2,1)} async-done(((bf16[512,2048]{1,0:T(8,128)(2,1)}), bf16[512,1024]{1,0:T(8,128)(2,1)}) %reduce-scatter.11.cloned.1.call-update) | async-done | bytes 1048592 | tf_op jit(solution)/shard_map/reduce_scatter | solution.py:98
  203.4 5.5 %convolution_convert_fusion = bf16[1024,2048]{1,0:T(8,128)(2,1)} fusion(bf16[1024,512]{1,0:T(8,128)(2,1)} %copy-done.14, bf16[2048,512]{1,0:T(8,128)(2,1)S(1)} %copy-done.11), kind=kOutput, calls=%fused_computation.6 | convolution fusion | flops 2149580800 | bytes 7340032 | tf_op jit(solution)/shard_map/dot_general | solution.py:30
  209.0 6.4 %copy.21 = bf16[1024,2048]{0,1:T(8,128)(2,1)} copy(bf16[1024,2048]{1,0:T(8,128)(2,1)} %convolution_convert_fusion) | data formatting | bytes 8388608
  215.4 1.6 copy-done.12
  217.0 5.5 %convolution_convert_fusion.1 = bf16[1024,2048]{1,0:T(8,128)(2,1)} fusion(bf16[1024,512]{1,0:T(8,128)(2,1)} %copy-done.13, bf16[512,2048]{1,0:T(8,128)(2,1)S(1)} %copy-done.12), kind=kOutput, calls=%fused_computation.7 | convolution fusion | flops 2149580800 | bytes 7340032 | tf_op jit(solution)/shard_map/dot_general | solution.py:64
  222.5 6.4 %copy.19 = bf16[1024,2048]{0,1:T(8,128)(2,1)} copy(bf16[1024,2048]{1,0:T(8,128)(2,1)} %convolution_convert_fusion.1) | data formatting | bytes 8388608
  229.0 6.4 %fusion = f32[1024,2048]{1,0:T(8,128)} fusion(bf16[1024,2048]{1,0:T(8,128)(2,1)} %all-gather.7.cloned.1.call-done, f32[1024]{0:T(1024)S(1)} %add_rsqrt_fusion, f32[1024]{0:T(1024)S(1)} %broadcast_multiply_fusion.2), kind=kLoop, calls=%fused_computation.2 | loop fusion | flops 6291456 | bytes 12591104 | tf_op jit(solution)/shard_map/mul | solution.py:58
  235.4 30.6 %all-reduce.6.cloned.1.call-done = (bf16[1024,512]{1,0:T(8,128)(2,1)}, bf16[512,1024]{1,0:T(8,128)(2,1)}) async-done(((bf16[1024,512]{1,0:T(8,128)(2,1)}, bf16[512,1024]{1,0:T(8,128)(2,1)}), (bf16[1024,512]{1,0:T(8,128)(2,1)}, bf16[512,1024]{1,0:T(8,128)(2,1)})) %all-reduce.6.cloned.1.call-update) | async-done | bytes 2097168 | tf_op jit(solution)/shard_map/psum | solution.py:103
  266.0 0.3 mul.177
  266.4 0.9 copy-done.4
  267.3 1.7 bitcast_multiply_fusion.1
  269.0 0.2 mul.180
  269.2 1.0 copy-done.3
  270.2 2.0 bitcast_multiply_fusion
  272.2 75.3 %reduce-scatter.15.cloned.1.call-done = bf16[128,1024]{1,0:T(8,128)(2,1)} async-done(((bf16[2048,1024]{1,0:T(8,128)(2,1)}), bf16[128,1024]{1,0:T(8,128)(2,1)}) %reduce-scatter.15.cloned.1.call-update) | async-done | bytes 262160
  347.4 1.1 copy.22
  348.6 79.2 %reduce-scatter.13.cloned.1.call-done = bf16[128,1024]{1,0:T(8,128)(2,1)} async-done(((bf16[2048,1024]{1,0:T(8,128)(2,1)}), bf16[128,1024]{1,0:T(8,128)(2,1)}) %reduce-scatter.13.cloned.1.call-update) | async-done | bytes 262160
  427.7 1.1 copy.20
  428.9 0.8 add_convert_fusion.4
  429.6 1.4 fusion.29
  431.0 10.4 %all-reduce.1 = (f32[128]{0:T(128)S(1)}, f32[128]{0:T(128)S(1)}) all-reduce(f32[128]{0:T(128)S(1)} %get-tuple-element.6, f32[128]{0:T(128)S(1)} %get-tuple-element.9), channel_id=1, replica_groups=mesh['rep'=4,'fsdp'=2,'tp'=16] {'rep'}, use_global_device_ids=true, to_apply=%region_13.0 | all-reduce | flops 256 | bytes 2048 | tf_op jit(solution)/shard_map/psum | solution.py:12
  441.5 3.0 all-reduce.2
  444.4 38.7 %all-reduce = (f32[1024]{0:T(1024)S(1)}, f32[1024]{0:T(1024)S(1)}) all-reduce(f32[1024]{0:T(1024)S(1)} %get-tuple-element.7, f32[1024]{0:T(1024)S(1)} %get-tuple-element.8), channel_id=1, replica_groups=mesh['rep'=4,'fsdp'=2,'tp'=16] {'tp'}, use_global_device_ids=true, to_apply=%region_7.0 | all-reduce | flops 2048 | bytes 16384 | tf_op jit(solution)/shard_map/psum | solution.py:84
  483.2 2.4 fusion.27
  (49 shorter events, 0.6 us)
Async XLA Ops:
  7.2 63.2 %all-gather.7.cloned.1.call-start = ((), (), s32[]{:S(2)}) async-start(), calls=%async_computation.4 | async-start | bytes 4456448 | tf_op jit(solution)/shard_map/all_gather | solution.py:39
  7.9 77.2 %all-gather.9.cloned.1.call-start = ((), (), s32[]{:S(2)}) async-start(), calls=%async_computation.5 | async-start | bytes 3145728 | tf_op jit(solution)/shard_map/all_gather | solution.py:47
  9.2 2.5 copy-start.8
  9.2 2.7 copy-start.2
  11.6 89.8 %all-gather.11.cloned.1.call-start = ((), (), s32[]{:S(2)}) async-start(), calls=%async_computation.6 | async-start | bytes 3145728 | tf_op jit(solution)/shard_map/all_gather | solution.py:48
  11.9 1.9 copy-start.10
  11.9 24.0 %copy-start.9 = (bf16[128]{0:T(256)(128)(2,1)S(1)}, bf16[128]{0:T(256)(128)(2,1)}, u32[]{:S(2)}) copy-start(bf16[128]{0:T(256)(128)(2,1)} %param.13) | copy-start | bytes 772
  11.9 43.6 %copy-start.7 = (s32[1024]{0:T(1024)S(1)}, s32[1024]{0:T(1024)}, u32[]{:S(2)}) copy-start(s32[1024]{0:T(1024)} %param.11) | copy-start | bytes 12292
  13.2 149.4 %all-gather.13.cloned.1.call-start = ((), (), s32[]{:S(2)}) async-start(), calls=%async_computation.7 | async-start | bytes 4456448 | tf_op jit(solution)/shard_map/all_gather | solution.py:40
  13.8 173.0 %reduce-scatter.9.cloned.1.call-start = ((), (), s32[]{:S(2)}) async-start(), calls=%async_computation.8 | async-start | bytes 3145728 | tf_op jit(solution)/shard_map/reduce_scatter | solution.py:95
  70.4 3.4 copy-start
  95.6 79.8 %copy-start.13 = (bf16[1024,512]{1,0:T(8,128)(2,1)}, bf16[1024,512]{1,0:T(8,128)(2,1)S(1)}, u32[]{:S(2)}) copy-start(bf16[1024,512]{1,0:T(8,128)(2,1)S(1)} %get-tuple-element.18) | copy-start | bytes 3145732
  162.5 8.1 %copy-start.1 = (bf16[1024,2048]{1,0:T(8,128)(2,1)S(1)}, bf16[1024,2048]{1,0:T(8,128)(2,1)}, u32[]{:S(2)}) copy-start(bf16[1024,2048]{1,0:T(8,128)(2,1)} %all-gather.7.cloned.1.call-done) | copy-start | bytes 12582916
  169.6 1.0 copy-start.14
  175.1 28.2 %reduce-scatter.11.cloned.1.call-start = ((), (), s32[]{:S(2)}) async-start(), calls=%async_computation.9 | async-start | bytes 3145728 | tf_op jit(solution)/shard_map/reduce_scatter | solution.py:98
  181.4 22.1 %copy-start.11 = (bf16[2048,512]{1,0:T(8,128)(2,1)S(1)}, bf16[2048,512]{1,0:T(8,128)(2,1)}, u32[]{:S(2)}) copy-start(bf16[2048,512]{1,0:T(8,128)(2,1)} %all-gather.9.cloned.1.call-done) | copy-start | bytes 6291460
  181.4 84.7 %all-reduce.6.cloned.1.call-start = ((), (), s32[]{:S(2)}) async-start(), calls=%async_computation.12 | async-start | bytes 4194304 | tf_op jit(solution)/shard_map/psum | solution.py:103
  203.4 144.1 %reduce-scatter.15.cloned.1.call-start = ((), (), s32[]{:S(2)}) async-start(), calls=%async_computation.11 | async-start | bytes 4456448
  215.3 1.6 copy-start.12
  215.4 212.4 %reduce-scatter.13.cloned.1.call-start = ((), (), s32[]{:S(2)}) async-start(), calls=%async_computation.10 | async-start | bytes 4456448
  266.0 1.2 copy-start.4
  269.0 1.2 copy-start.3
  270.2 158.7 %copy-start.5 = (bf16[1024,128]{1,0:T(8,128)(2,1)S(1)}, bf16[1024,128]{1,0:T(8,128)(2,1)}, u32[]{:S(2)}) copy-start(bf16[1024,128]{1,0:T(8,128)(2,1)} %param.9) | copy-start | bytes 786436
  272.2 211.0 %copy-start.6 = (bf16[1024,128]{1,0:T(8,128)(2,1)S(1)}, bf16[1024,128]{1,0:T(8,128)(2,1)}, u32[]{:S(2)}) copy-start(bf16[1024,128]{1,0:T(8,128)(2,1)} %param.10) | copy-start | bytes 786436
Sparse Core Ops, SparseCore 0:
  10.1 60.2 all-gather.6
  72.6 12.4 all-gather.8
  86.8 14.6 all-gather.10
  103.4 59.0 all-gather.12
  175.3 11.4 reduce-scatter.8
  189.6 13.6 reduce-scatter.10
  205.8 60.2 all-reduce.5
  269.7 77.6 reduce-scatter.14
  350.8 76.9 reduce-scatter.12
